TPU v7x, 256 devices: a whole 4x4x8 slice. The times are simulated.
256 devices in a mesh: dp: 8 (over x_hi, y), seq: 32 (over x_lo, z, core).
Axes of the slice: x: 4 (x_hi: 2, x_lo: 2; x = x_hi * 2 + x_lo), y: 4, z: 8, core: 2. Of those that a mesh axis runs over, the one named last changes fastest.
Arguments:
- tokens: bfloat16 [8, 12288, 2048], P('dp', 'seq'), may hold values from -32 to 32
- w_qkv: bfloat16 [2048, 3072], P(('dp', 'seq')), may hold values from -1 to 1
- w_out: bfloat16 [1024, 2048], P(('dp', 'seq')), may hold values from -0.1875 to 0.1875
Outputs:
- mixed: bfloat16 [8, 12288, 2048], P('dp', 'seq')
All inputs are finite; a program needn't handle non-finite values.
Results may differ from a plain program's by a relative error of at most 0.007.
Values may be sent and summed in bfloat16 or wider, within the bound.
No kernel may reach another device: no remote copies, remote signals or barrier semaphores. Data moves between devices by JAX's collectives and lax.ppermute only.
A program may use at most 64 MiB of HBM per device.

v0:
```python
import math
import jax
import jax.numpy as jnp
from jax import lax
from jax.sharding import PartitionSpec as P

HEADS = 8
HEAD_DIM = 128
COLS = 96


def attend(query, keys, values, allowed):
    scores = jnp.einsum(
        "shqd,shkd->shqk", query, keys, preferred_element_type=jnp.float32
    ) / math.sqrt(query.shape[-1])
    scores = jnp.where(allowed, scores, -jnp.inf)
    top = jnp.max(scores, axis=-1, keepdims=True)
    expo = jnp.exp(scores - top)
    weights = (expo / jnp.sum(expo, axis=-1, keepdims=True)).astype(jnp.bfloat16)
    return jnp.einsum(
        "shqk,shkd->shqd", weights, values, preferred_element_type=jnp.float32
    ).astype(jnp.bfloat16)


def add_rows(left, piece):
    return jnp.dot(left, piece, preferred_element_type=jnp.float32)


def column_heads(packed):
    seq_count, grid_rows, local_cols, count, width = packed.shape
    length = grid_rows * local_cols
    flat = packed.reshape(seq_count, length, count, 3, width // 3)
    flat = jnp.transpose(flat, (0, 2, 3, 1, 4))
    places = jnp.arange(length)
    allowed = (places[:, None] % local_cols == places[None, :] % local_cols) & (
        places[:, None] >= places[None, :]
    )
    result = attend(flat[:, :, 0], flat[:, :, 1], flat[:, :, 2], allowed)
    result = jnp.transpose(result, (0, 2, 1, 3)).reshape(
        seq_count, grid_rows, local_cols, count, width // 3
    )
    return lax.all_to_all(result, "seq", split_axis=1, concat_axis=2, tiled=True)


def on_device(tokens, w_qkv, w_out):
    seq_count, tok_count, width = tokens.shape
    flat = tokens.reshape(seq_count * tok_count, width)
    half = HEADS // 2
    qkv = add_rows(flat, lax.all_gather(w_qkv, ("dp", "seq"), axis=0, tiled=True))
    qkv = qkv.astype(jnp.bfloat16).reshape(seq_count, tok_count, HEADS, 3, HEAD_DIM)
    col_packed = qkv[:, :, half:].reshape(seq_count, tok_count // COLS, COLS, half, 3 * HEAD_DIM)
    col_out = column_heads(
        lax.all_to_all(col_packed, "seq", split_axis=2, concat_axis=1, tiled=True)
    )
    col_out = col_out.reshape(seq_count, tok_count, half, HEAD_DIM)
    row_part = jnp.transpose(qkv[:, :, :half], (0, 2, 3, 1, 4))
    places = jnp.arange(tok_count)
    row_mask = (places[:, None] // COLS == places[None, :] // COLS) & (
        places[:, None] >= places[None, :]
    )
    row_out = attend(row_part[:, :, 0], row_part[:, :, 1], row_part[:, :, 2], row_mask)
    row_out = jnp.transpose(row_out, (0, 2, 1, 3))
    heads_out = jnp.concatenate([row_out, col_out], axis=2).reshape(
        seq_count * tok_count, HEADS * HEAD_DIM
    )
    mixed = add_rows(heads_out, lax.all_gather(w_out, ("dp", "seq"), axis=0, tiled=True))
    return mixed.astype(jnp.bfloat16).reshape(seq_count, tok_count, w_out.shape[1])


def solution(mesh):
    in_specs = (P("dp", "seq", None), P(("dp", "seq"), None), P(("dp", "seq"), None))
    out_specs = P("dp", "seq", None)
    return jax.shard_map(
        on_device, mesh=mesh, in_specs=in_specs, out_specs=out_specs, check_vma=False
    )
```

profile of v0, /device:TPU:32, one launch (start us, length us, event | category | flops | bytes accessed | tf_op | source)
XLA Modules:
  0.0 879.4 jit_solution(4951368546532255029)
XLA Ops:
  6.5 0.7 all-gather.4.cloned.1.call-update
  7.3 0.7 all-gather.6.cloned.1.call-update
  8.0 427.3 %all-gather.4.cloned.1.call-done = bf16[2048,3072]{1,0:T(8,128)(2,1)} async-done(((bf16[8,3072]{1,0:T(8,128)(2,1)}), bf16[2048,3072]{1,0:T(8,128)(2,1)}) %all-gather.4.cloned.1.call-update) | async-done | bytes 12582928 | tf_op jit(solution)/shard_map/all_gather | solution.py:49
  435.3 10.9 %convolution_convert_fusion = bf16[384,3072]{1,0:T(8,128)(2,1)} fusion(bf16[2048,3072]{1,0:T(8,128)(2,1)} %all-gather.4.cloned.1.call-done, bf16[1,384,2048]{2,1,0:T(8,128)(2,1)S(1)} %copy-done), kind=kOutput, calls=%fused_computation.2 | convolution fusion | flops 4833017856 | bytes 16515072 | tf_op jit(solution)/shard_map/dot_general | solution.py:26
  446.1 4.3 copy.33
  450.4 3.4 fusion.36
  453.8 3.3 reshape.184
  457.1 2.4 copy.38
  459.5 6.5 all-to-all-start
  466.2 32.2 %all-to-all-done = bf16[1,4,96,4,384]{4,1,3,0,2:T(4,128)(2,1)S(1)} async-done(((bf16[1,4,96,4,384]{4,1,3,0,2:T(4,128)(2,1)}), bf16[1,4,96,4,384]{4,1,3,0,2:T(4,128)(2,1)S(1)}, u32[]{:S(2)}, u32[]{:S(2)}) %all-to-all-start) | async-done | bytes 1179680 | tf_op jit(solution)/shard_map/all_to_all | solution.py:53
  498.4 0.5 copy.39
  498.9 1.4 copy.40
  500.3 3.4 reshape.174
  503.7 1.4 copy.55
  505.1 2.1 fusion.37
  507.2 1.3 fusion.7
  508.5 1.1 copy.43
  509.5 4.5 all-to-all-start.1
  514.2 339.7 %all-gather.6.cloned.1.call-done = bf16[256,4,2048]{2,1,0:T(4,128)(2,1)} async-done(((bf16[1,4,2048]{2,1,0:T(4,128)(2,1)}), bf16[256,4,2048]{2,1,0:T(4,128)(2,1)}) %all-gather.6.cloned.1.call-update) | async-done | bytes 4194320 | tf_op jit(solution)/shard_map/all_gather | solution.py:66
  854.0 6.9 reshape.183
  860.9 1.4 copy.53
  862.3 2.1 fusion.38
  864.5 2.1 fusion.6
  867.4 5.2 fusion.2
  (21 shorter events, 1.1 us)
Async XLA Ops:
  6.5 428.7 %copy-start = (bf16[1,384,2048]{2,1,0:T(8,128)(2,1)S(1)}, bf16[1,384,2048]{2,1,0:T(8,128)(2,1)}, u32[]{:S(2)}) copy-start(bf16[1,384,2048]{2,1,0:T(8,128)(2,1)} %param.3) | copy-start | bytes 4718596
  6.5 428.7 %all-gather.4.cloned.1.call-start = ((), (), s32[]{:S(2)}) async-start(), calls=%async_computation.2 | async-start | bytes 12632064 | tf_op jit(solution)/shard_map/all_gather | solution.py:49
  7.3 846.7 %all-gather.6.cloned.1.call-start = ((), (), s32[]{:S(2)}) async-start(), calls=%async_computation.3 | async-start | bytes 4210688 | tf_op jit(solution)/shard_map/all_gather | solution.py:66
  459.5 38.9 %all-to-all-start = ((bf16[1,4,96,4,384]{4,1,3,0,2:T(4,128)(2,1)}), bf16[1,4,96,4,384]{4,1,3,0,2:T(4,128)(2,1)S(1)}, u32[]{:S(2)}, u32[]{:S(2)}) async-start(bf16[1,4,96,4,384]{4,1,3,0,2:T(4,128)(2,1)} %copy.38), calls=%async_computation | async-start | bytes 2359296 | tf_op jit(solution)/shard_map/all_to_all | solution.py:53
  505.1 2.1 copy-start.3
  509.5 357.1 %all-to-all-start.1 = ((bf16[1,128,3,4,128]{4,3,2,0,1:T(4,128)(2,1)}), bf16[1,128,3,4,128]{4,3,2,0,1:T(4,128)(2,1)S(1)}, u32[]{:S(2)}, u32[]{:S(2)}) async-start(bf16[1,128,3,4,128]{4,3,2,0,1:T(4,128)(2,1)} %bitcast.17), calls=%async_computation.1 | async-start | bytes 786432 | tf_op jit(solution)/shard_map/all_to_all | solution.py:42
  514.2 348.1 %copy-start.4 = (pred[384,384]{0,1:T(8,128)(4,1)}, pred[384,384]{0,1:T(8,128)(4,1)S(1)}, u32[]{:S(2)}) copy-start(pred[384,384]{0,1:T(8,128)(4,1)S(1)} %fusion.15) | copy-start | bytes 442372
  514.2 346.6 %copy-start.1 = (bf16[1,384,4,3,128]{1,4,3,2,0:T(8,128)(2,1)S(1)}, bf16[1,384,4,3,128]{1,4,3,2,0:T(8,128)(2,1)}, u32[]{:S(2)}) copy-start(bf16[1,384,4,3,128]{1,4,3,2,0:T(8,128)(2,1)} %get-tuple-element.5) | copy-start | bytes 3538948
  862.3 2.1 copy-start.2
Sparse Core Ops, SparseCore 0:
  9.2 425.9 all-gather.3
  437.1 416.7 all-gather.5
where the time goes:
time: 880 us; the launch traced here: 879 us
  waiting for transfers between devices  801 us (91%)
  local copies, waits for them, and re-layouts  30.1 us (3%)
  matrix products  23.7 us (3%)
  between operations  13.5 us (2%)
  starting transfers between devices  11.1 us (1%)
    all_gather x1, waiting for transfers between devices, on_device(): lax.all_gather(w_qkv, ('dp', 'seq'), axis=0, tiled=True)  427 us
    all_gather x1, waiting for transfers between devices, on_device(): lax.all_gather(w_out, ('dp', 'seq'), axis=0, tiled=True)  340 us
    all_to_all x1, waiting for transfers between devices, on_device(): lax.all_to_all(col_packed, 'seq', split_axis=2, concat_axis=1, tiled=True)  32.2 us
  transfers between devices with their start and end apart: 4, of which 3 were waited for; matrix products, arithmetic and copies ran while one was open for 5% of the time, Pallas kernels for 0%

commit v1 on v0

--- a/solution.py
+++ b/solution.py
@@ -50,7 +50,12 @@
     qkv = qkv.astype(jnp.bfloat16).reshape(seq_count, tok_count, HEADS, 3, HEAD_DIM)
     col_packed = qkv[:, :, half:].reshape(seq_count, tok_count // COLS, COLS, half, 3 * HEAD_DIM)
     col_out = column_heads(
-        lax.all_to_all(col_packed, "seq", split_axis=2, concat_axis=1, tiled=True)
+        jnp.concatenate(
+            lax.all_to_all(
+                jnp.stack(jnp.split(col_packed, lax.axis_size("seq"), axis=2)), "seq", 0, 0
+            ),
+            axis=1,
+        )
     )
     col_out = col_out.reshape(seq_count, tok_count, half, HEAD_DIM)
     row_part = jnp.transpose(qkv[:, :, :half], (0, 2, 3, 1, 4))

time: 880 us -> 879 us (level)
  waiting for transfers between devices: 801 us -> 693 us
  local copies, waits for them, and re-layouts: 30.1 us -> 135 us
    all_gather x1, waiting for transfers between devices: 340 us -> 234 us  [on_device(): lax.all_gather(w_out, ('dp', 'seq'), axis=0, tiled=True)]
    unnamed x12 -> x107, local copies, waits for them, and re-layouts: 8.37 us -> 94 us
    split x0 -> x2, local copies, waits for them, and re-layouts: none -> 31.5 us  [on_device(): jnp.split(col_packed, lax.axis_size('seq'), axis=2)]
  transfers between devices with their start and end apart: 4 -> 4, of which waited for: 3 -> 3; matrix products, arithmetic and copies ran while one was open for 5% -> 17% of each run, Pallas kernels for 0% -> 0%
where the time goes in v1:
time: 879 us; the launch traced here: 876 us
  waiting for transfers between devices  693 us (79%)
  local copies, waits for them, and re-layouts  135 us (15%)
  matrix products  20.5 us (2%)
  between operations  13.9 us (2%)
  starting transfers between devices  13 us (1%)
    all_gather x1, waiting for transfers between devices, on_device(): lax.all_gather(w_qkv, ('dp', 'seq'), axis=0, tiled=True)  427 us
    all_gather x1, waiting for transfers between devices, on_device(): lax.all_gather(w_out, ('dp', 'seq'), axis=0, tiled=True)  234 us
    unnamed x107, local copies, waits for them, and re-layouts  94 us
    split x2, local copies, waits for them, and re-layouts, on_device(): jnp.split(col_packed, lax.axis_size('seq'), axis=2)  31.5 us
    all_to_all x1, waiting for transfers between devices, on_device(): lax.all_to_all(jnp.stack(jnp.split(col_packed, lax.axis_size('seq'), axis...  30.4 us
  transfers between devices with their start and end apart: 4, of which 3 were waited for; matrix products, arithmetic and copies ran while one was open for 17% of the time, Pallas kernels for 0%

profile of v1, /device:TPU:32, one launch (start us, length us, event | category | flops | bytes accessed | tf_op | source)
XLA Modules:
  0.0 876.1 jit_solution(8757345693403767040)
XLA Ops:
  8.0 427.3 %all-gather.4.cloned.1.call-done = bf16[2048,3072]{1,0:T(8,128)(2,1)} async-done(((bf16[8,3072]{1,0:T(8,128)(2,1)}), bf16[2048,3072]{1,0:T(8,128)(2,1)}) %all-gather.4.cloned.1.call-update) | async-done | bytes 12582928 | tf_op jit(solution)/shard_map/all_gather | solution.py:49
  435.3 10.8 %convolution_convert_fusion = bf16[384,3072]{1,0:T(8,128)(2,1)} fusion(bf16[2048,3072]{1,0:T(8,128)(2,1)} %all-gather.4.cloned.1.call-done, bf16[1,384,2048]{2,1,0:T(8,128)(2,1)S(1)} %copy-done), kind=kOutput, calls=%fused_computation.2 | convolution fusion | flops 4833017856 | bytes 16515072 | tf_op jit(solution)/shard_map/dot_general | solution.py:26
  446.1 3.0 copy.20
  451.6 12.6 %fusion.38 = (bf16[1,4,3,4,384]{2,1,4,3,0:T(4,128)(2,1)S(1)}, bf16[1,4,3,4,384]{2,1,4,3,0:T(4,128)(2,1)}, bf16[1,4,3,4,384]{2,1,4,3,0:T(4,128)(2,1)}, bf16[1,4,3...) fusion(bf16[1,4,96,4,384]{2,1,4,3,0:T(4,128)(2,1)S(1)} %reshape.179), kind=kLoop, calls=%fused_computation.91 | loop fusion | bytes 958464 | tf_op jit(solution)/shard_map/split | solution.py:55
  464.3 18.9 %fusion.37 = (bf16[1,4,3,4,384]{2,1,4,3,0:T(4,128)(2,1)}, bf16[1,4,3,4,384]{2,1,4,3,0:T(4,128)(2,1)}, bf16[1,4,3,4,384]{2,1,4,3,0:T(4,128)(2,1)}, bf16[1,4,3,4,3...) fusion(bf16[1,4,96,4,384]{2,1,4,3,0:T(4,128)(2,1)S(1)} %reshape.179), kind=kLoop, calls=%fused_computation.90 | loop fusion | bytes 1400832 | tf_op jit(solution)/shard_map/split | solution.py:55
  483.2 2.9 copy.38
  490.5 2.9 copy.41
  493.4 2.8 copy.42
  497.1 2.9 copy.44
  500.0 2.8 copy.45
  508.8 3.5 copy.47
  512.3 3.4 copy.48
  521.0 3.5 copy.52
  528.0 3.5 copy.55
  535.0 3.5 copy.58
  542.0 3.5 copy.61
  547.3 2.9 copy.64
  552.0 2.9 copy.67
  571.4 6.6 all-to-all-start
  578.1 30.4 %all-to-all-done = bf16[32,1,4,3,4,384]{5,4,3,2,1,0:T(4,128)(2,1)S(1)} async-done(((bf16[32,1,4,3,4,384]{5,4,3,2,1,0:T(4,128)(2,1)}), bf16[32,1,4,3,4,384]{5,4,3,2,1,0:T(4,128)(2,1)S(1)}, u32[]{:S(2)}, u32[]{:S(2)}) %all-to-all-start) | async-done | bytes 1179680 | tf_op jit(solution)/shard_map/all_to_all | solution.py:54
  612.7 6.4 all-to-all-start.1
  619.2 234.1 %all-gather.6.cloned.1.call-done = bf16[256,4,2048]{2,1,0:T(4,128)(2,1)} async-done(((bf16[1,4,2048]{2,1,0:T(4,128)(2,1)}), bf16[256,4,2048]{2,1,0:T(4,128)(2,1)}) %all-gather.6.cloned.1.call-update) | async-done | bytes 4194320 | tf_op jit(solution)/shard_map/all_gather | solution.py:71
  853.3 6.9 reshape.178
  863.9 5.3 fusion.2
  (117 shorter events, 58.6 us)
Async XLA Ops:
  6.5 428.7 %copy-start = (bf16[1,384,2048]{2,1,0:T(8,128)(2,1)S(1)}, bf16[1,384,2048]{2,1,0:T(8,128)(2,1)}, u32[]{:S(2)}) copy-start(bf16[1,384,2048]{2,1,0:T(8,128)(2,1)} %param.3) | copy-start | bytes 4718596
  6.5 428.7 %all-gather.4.cloned.1.call-start = ((), (), s32[]{:S(2)}) async-start(), calls=%async_computation.2 | async-start | bytes 12632064 | tf_op jit(solution)/shard_map/all_gather | solution.py:49
  7.3 846.0 %all-gather.6.cloned.1.call-start = ((), (), s32[]{:S(2)}) async-start(), calls=%async_computation.3 | async-start | bytes 4210688 | tf_op jit(solution)/shard_map/all_gather | solution.py:71
  483.2 6.4 copy-start.5
  490.5 5.8 copy-start.4
  497.1 5.8 copy-start.3
  508.8 6.9 copy-start.2
  517.5 1.8 copy-start.18
  519.2 5.3 copy-start.17
  521.0 5.3 copy-start.16
  526.3 5.3 copy-start.15
  528.0 5.3 copy-start.14
  533.3 5.3 copy-start.13
  535.0 5.3 copy-start.12
  540.3 5.3 copy-start.11
  542.0 4.4 copy-start.10
  546.4 3.8 copy-start.9
  547.3 3.8 copy-start.8
  551.1 3.8 copy-start.7
  552.0 3.8 copy-start.6
  571.4 37.1 %all-to-all-start = ((bf16[32,1,4,3,4,384]{5,4,3,2,1,0:T(4,128)(2,1)}), bf16[32,1,4,3,4,384]{5,4,3,2,1,0:T(4,128)(2,1)S(1)}, u32[]{:S(2)}, u32[]{:S(2)}) async-start(bf16[32,1,4,3,4,384]{5,4,3,2,1,0:T(4,128)(2,1)} %copy.25), calls=%async_computation | async-start | bytes 2359296 | tf_op jit(solution)/shard_map/all_to_all | solution.py:54
  612.7 250.5 %all-to-all-start.1 = ((bf16[1,128,3,4,128]{4,3,2,0,1:T(4,128)(2,1)}), bf16[1,128,3,4,128]{4,3,2,0,1:T(4,128)(2,1)S(1)}, u32[]{:S(2)}, u32[]{:S(2)}) async-start(bf16[1,128,3,4,128]{4,3,2,0,1:T(4,128)(2,1)} %bitcast.47), calls=%async_computation.1 | async-start | bytes 786432 | tf_op jit(solution)/shard_map/all_to_all | solution.py:42
  619.2 241.0 %copy-start.19 = (bf16[1,384,4,3,128]{1,4,3,2,0:T(8,128)(2,1)S(1)}, bf16[1,384,4,3,128]{1,4,3,2,0:T(8,128)(2,1)}, u32[]{:S(2)}) copy-start(bf16[1,384,4,3,128]{1,4,3,2,0:T(8,128)(2,1)} %get-tuple-element.5) | copy-start | bytes 3538948
  863.9 5.3 copy-start.1
  (1 other events, 1.4 us)
Sparse Core Ops, SparseCore 0:
  9.2 425.9 all-gather.3
  437.1 416.1 all-gather.5
